TPU v7x, 512 devices: a whole 4x8x8 slice. The times are simulated.
512 devices in a mesh: section: 2 (over z_lo), tensor: 4 (over x), seq: 64 (over y, z_hi, core).
Axes of the slice: x: 4, y: 8, z: 8 (z_hi: 4, z_lo: 2; z = z_hi * 2 + z_lo), core: 2. Of those that a mesh axis runs over, the one named last changes fastest.
Arguments:
- tokens: bfloat16 [16384, 2560], P('seq', ('section', 'tensor')), may hold values from -6 to 6
- w_query: bfloat16 [2560, 2048], P(None, ('section', 'tensor')), may hold values from -0.125 to 0.125
- w_keyval: bfloat16 [2560, 2048], P(None, ('section', 'tensor')), may hold values from -0.125 to 0.125
- w_out: bfloat16 [2048, 2560], P(('section', 'tensor')), may hold values from -0.125 to 0.125
- w_gateup: bfloat16 [2560, 2, 5120], P('seq', None, ('section', 'tensor')), may hold values from -0.125 to 0.125
- attn_gain: float32 [2560], replicated, may hold values from 0.1 to 1.9
- post_gain: float32 [2560], replicated, may hold values from 0.1 to 1.9
- mlp_gain: float32 [2560], replicated, may hold values from 0.1 to 1.9
- query_gain: float32 [256], replicated, may hold values from 0.7 to 6.5
- key_gain: float32 [256], replicated, may hold values from 0.7 to 6.5
- prompt_lengths: int32 [8], replicated, may hold values from 1 to 4096, as said below
- page_slots: int32 [128], P('seq'), may hold values from 0 to 1, as said below
Outputs:
- hidden: bfloat16 [16384, 5120], P('seq', ('section', 'tensor'))
- page_cache: bfloat16 [128, 128, 2048], P('seq', None, ('section', 'tensor'))
Inputs may be any that keep to these rules, and one draw needn't show every extreme that they name: `prompt_lengths`: each prompt has at least one token; they sum to 16384; one prompt has exactly 4096 tokens and begins strictly inside a token block. `page_slots`: within each aligned group of 2 pages (the pages of one token block) the slots are a permutation of 0 to 1.
All inputs are finite; a program needn't handle non-finite values.
Results may differ from a plain program's by a relative error of at most 0.01.
The roundings to bfloat16 on the way count: a program that leaves them out, or rounds other values in their place, can miss the bound.
Values may be sent and summed in bfloat16 or wider, within the bound.
No kernel may reach another device: no remote copies, remote signals or barrier semaphores. Data moves between devices by JAX's collectives and lax.ppermute only.
A program may use at most 64 MiB of HBM per device.

v0:
```python
import jax
import jax.numpy as jnp
from jax import lax
from jax.sharding import PartitionSpec as P

REACH = 16
NORM_EPS = 1e-06
ROPE_BASE = 1000000.0
ROPE_FACTOR = 8.0


def swapped(value, axis, bit):
    mask = 2**bit
    pairs = [(source, source ^ mask) for source in range(lax.axis_size(axis))]
    return lax.ppermute(value, axis, pairs)


def shifted(block, axis, distance):
    devices = range(lax.axis_size(axis))
    route = [(i - distance, i) for i in devices if i - distance in devices]
    return lax.ppermute(block, axis, route)


def rms_norm(values, weights):
    values = values.astype(jnp.float32)
    inverse = lax.rsqrt(jnp.mean(values * values, axis=-1, keepdims=True) + NORM_EPS)
    return values * inverse * weights


def angle_tables(position, head_width):
    halfway = head_width // 2
    exponent = jnp.arange(halfway, dtype=jnp.float32) * (2.0 / head_width)
    frequency = ROPE_BASE ** (-exponent)
    angles = (position.astype(jnp.float32) / ROPE_FACTOR)[:, None] * frequency[None, :]
    return (jnp.cos(angles), jnp.sin(angles))


def rotary(values, cosine_table, sine_table):
    halfway = values.shape[-1] // 2
    lower_half = values[..., :halfway]
    upper_half = values[..., halfway:]
    return jnp.concatenate(
        [
            lower_half * cosine_table - upper_half * sine_table,
            upper_half * cosine_table + lower_half * sine_table,
        ],
        axis=-1,
    )


def local(
    tokens,
    w_query,
    w_keyval,
    w_out,
    w_gateup,
    attn_gain,
    post_gain,
    mlp_gain,
    query_gain,
    key_gain,
    prompt_lengths,
    page_slots,
):
    row_count = tokens.shape[0]
    head_width = w_query.shape[1]
    halfway = head_width // 2
    unit_count = w_gateup.shape[2]
    span_blocks = min(REACH, lax.axis_size("seq") // 2)
    features = lax.all_gather(tokens, ("section", "tensor"), axis=1, tiled=True)
    first_row = lax.axis_index("seq") * row_count
    prompt_ends = jnp.cumsum(prompt_lengths)
    prompt_starts = prompt_ends - prompt_lengths
    query_index = first_row + jnp.arange(row_count, dtype=jnp.int32)
    query_segment = jnp.sum(
        (prompt_ends[None, :] <= query_index[:, None]).astype(jnp.int32), axis=1
    )
    chosen = query_segment[:, None] == jnp.arange(prompt_ends.shape[0], dtype=jnp.int32)[None, :]
    query_position = query_index - jnp.sum(jnp.where(chosen, prompt_starts[None, :], 0), axis=1)
    cosine_table, sine_table = angle_tables(query_position, head_width)
    normed = rms_norm(features, attn_gain).astype(jnp.bfloat16)
    queries = jnp.dot(normed, w_query, preferred_element_type=jnp.float32)
    queries = rotary(rms_norm(queries, query_gain), cosine_table, sine_table).astype(jnp.bfloat16)
    own_half = jnp.dot(normed, w_keyval, preferred_element_type=jnp.float32).astype(jnp.bfloat16)
    other_half = swapped(own_half, "tensor", 0)
    is_lower = lax.axis_index("tensor") % 2 == 0
    lower_part = jnp.where(is_lower, own_half, other_half)
    upper_part = jnp.where(is_lower, other_half, own_half)
    raw_keys = jnp.concatenate([lower_part[:, :halfway], upper_part[:, :halfway]], axis=1)
    values_full = jnp.concatenate([lower_part[:, halfway:], upper_part[:, halfway:]], axis=1)
    keys_full = rotary(rms_norm(raw_keys, key_gain), cosine_table, sine_table).astype(jnp.bfloat16)
    own_keys = jnp.where(is_lower, keys_full[:, :halfway], keys_full[:, halfway:])
    page_rows = jnp.concatenate([own_keys, own_half[:, halfway:]], axis=1)
    pages_here = page_slots.shape[0]
    page_rows = page_rows.reshape(pages_here, row_count // pages_here, head_width)
    page_cache = jnp.zeros_like(page_rows).at[page_slots].set(page_rows)
    key_block = jnp.stack([keys_full, values_full])
    received = [key_block]
    for distance in range(1, span_blocks + 1):
        received.append(shifted(key_block, "seq", distance))
    window_stack = jnp.stack(received)
    all_keys = window_stack[:, 0].reshape(-1, head_width)
    all_values = window_stack[:, 1].reshape(-1, head_width)
    offsets = (jnp.arange(span_blocks + 1, dtype=jnp.int32) * row_count)[:, None]
    key_index = (first_row - offsets + jnp.arange(row_count, dtype=jnp.int32)[None, :]).reshape(-1)
    key_segment = jnp.sum((prompt_ends[None, :] <= key_index[:, None]).astype(jnp.int32), axis=1)
    key_segment = jnp.where(key_index >= 0, key_segment, -1)
    allowed = (key_segment[None, :] == query_segment[:, None]) & (
        key_index[None, :] <= query_index[:, None]
    )
    scores = lax.dot_general(
        queries, all_keys, (((1,), (1,)), ((), ())), preferred_element_type=jnp.float32
    ) * head_width ** (-0.5)
    scores = jnp.where(allowed, scores, -jnp.inf)
    row_max = jnp.max(scores, axis=1, keepdims=True)
    exponent_terms = jnp.exp(scores - row_max)
    weights_low = (exponent_terms / jnp.sum(exponent_terms, axis=1, keepdims=True)).astype(
        jnp.bfloat16
    )
    attention_out = jnp.dot(weights_low, all_values, preferred_element_type=jnp.float32).astype(
        jnp.bfloat16
    )
    head_terms = jnp.dot(attention_out, w_out, preferred_element_type=jnp.float32)
    attended = lax.psum(head_terms, ("section", "tensor"))
    residual = features.astype(jnp.float32) + rms_norm(attended, post_gain)
    ffn_input = rms_norm(residual, mlp_gain).astype(jnp.bfloat16)
    row_piece = lax.all_gather(w_gateup, "seq", axis=0, tiled=True)
    piece_rows = row_piece.shape[0]
    projected = jnp.dot(
        ffn_input, row_piece.reshape(piece_rows, 2 * unit_count), preferred_element_type=jnp.float32
    )
    hidden = (
        jax.nn.gelu(projected[:, :unit_count], approximate=True) * projected[:, unit_count:]
    ).astype(jnp.bfloat16)
    return (hidden, page_cache)


def solution(mesh):
    return jax.shard_map(
        local,
        mesh=mesh,
        in_specs=(
            P("seq", ("section", "tensor")),
            P(None, ("section", "tensor")),
            P(None, ("section", "tensor")),
            P(("section", "tensor"), None),
            P("seq", None, ("section", "tensor")),
            P(),
            P(),
            P(),
            P(),
            P(),
            P(),
            P("seq"),
        ),
        out_specs=(P("seq", ("section", "tensor")), P("seq", None, ("section", "tensor"))),
        check_vma=False,
    )
```

profile of v0, /device:TPU:8, one launch (start us, length us, event | category | flops | bytes accessed | tf_op | source)
XLA Modules:
  0.0 404.8 jit_solution(14164455643297318080)
XLA Ops:
  10.7 49.9 %all-gather.3.cloned.1.call-done = bf16[256,2560]{0,1:T(8,128)(2,1)} async-done(((bf16[256,320]{0,1:T(8,128)(2,1)}), bf16[256,2560]{0,1:T(8,128)(2,1)}) %all-gather.3.cloned.1.call-update) | async-done | bytes 1310736 | tf_op jit(solution)/shard_map/all_gather | solution.py:70
  67.6 4.0 collective-permute-done
  75.0 4.6 %collective-permute-start.2 = (bf16[2,256,256]{1,2,0:T(8,128)(2,1)S(1)}, bf16[2,256,256]{1,2,0:T(8,128)(2,1)S(1)}, u32[]{:S(2)}, u32[]{:S(2)}) collective-permute-start(bf16[2,256,256]{1,2,0:T(8,128)(2,1)S(1)} %pad_maximum_fusion), channel_id=1, source_target_pairs={{0,2},{1,3},{2,4},{3,5},{4,6},{5,7},{6,8},{7,9},{8,10},{9,11},{10,... | collective-permute-start | bytes 786440 | tf_op jit(solution)/shard_map/ppermute | solution.py:21
  79.6 5.3 %collective-permute-start.3 = (bf16[2,256,256]{1,2,0:T(8,128)(2,1)S(1)}, bf16[2,256,256]{1,2,0:T(8,128)(2,1)S(1)}, u32[]{:S(2)}, u32[]{:S(2)}) collective-permute-start(bf16[2,256,256]{1,2,0:T(8,128)(2,1)S(1)} %pad_maximum_fusion), channel_id=1, source_target_pairs={{0,3},{1,4},{2,5},{3,6},{4,7},{5,8},{6,9},{7,10},{8,11},{9,12},{10... | collective-permute-start | bytes 786440 | tf_op jit(solution)/shard_map/ppermute | solution.py:21
  84.9 5.4 %collective-permute-start.4 = (bf16[2,256,256]{1,2,0:T(8,128)(2,1)S(1)}, bf16[2,256,256]{1,2,0:T(8,128)(2,1)S(1)}, u32[]{:S(2)}, u32[]{:S(2)}) collective-permute-start(bf16[2,256,256]{1,2,0:T(8,128)(2,1)S(1)} %pad_maximum_fusion), channel_id=1, source_target_pairs={{0,4},{1,5},{2,6},{3,7},{4,8},{5,9},{6,10},{7,11},{8,12},{9,13},{1... | collective-permute-start | bytes 786440 | tf_op jit(solution)/shard_map/ppermute | solution.py:21
  90.3 4.8 %collective-permute-start.5 = (bf16[2,256,256]{1,2,0:T(8,128)(2,1)S(1)}, bf16[2,256,256]{1,2,0:T(8,128)(2,1)S(1)}, u32[]{:S(2)}, u32[]{:S(2)}) collective-permute-start(bf16[2,256,256]{1,2,0:T(8,128)(2,1)S(1)} %pad_maximum_fusion), channel_id=1, source_target_pairs={{0,5},{1,6},{2,7},{3,8},{4,9},{5,10},{6,11},{7,12},{8,13},{9,14},{... | collective-permute-start | bytes 786440 | tf_op jit(solution)/shard_map/ppermute | solution.py:21
  95.1 6.0 %collective-permute-start.6 = (bf16[2,256,256]{1,2,0:T(8,128)(2,1)S(1)}, bf16[2,256,256]{1,2,0:T(8,128)(2,1)S(1)}, u32[]{:S(2)}, u32[]{:S(2)}) collective-permute-start(bf16[2,256,256]{1,2,0:T(8,128)(2,1)S(1)} %pad_maximum_fusion), channel_id=1, source_target_pairs={{0,6},{1,7},{2,8},{3,9},{4,10},{5,11},{6,12},{7,13},{8,14},{9,15},... | collective-permute-start | bytes 786440 | tf_op jit(solution)/shard_map/ppermute | solution.py:21
  101.2 18.7 %collective-permute-start.7 = (bf16[2,256,256]{1,2,0:T(8,128)(2,1)S(1)}, bf16[2,256,256]{1,2,0:T(8,128)(2,1)S(1)}, u32[]{:S(2)}, u32[]{:S(2)}) collective-permute-start(bf16[2,256,256]{1,2,0:T(8,128)(2,1)S(1)} %pad_maximum_fusion), channel_id=1, source_target_pairs={{0,7},{1,8},{2,9},{3,10},{4,11},{5,12},{6,13},{7,14},{8,15},{9,16}... | collective-permute-start | bytes 786440 | tf_op jit(solution)/shard_map/ppermute | solution.py:21
  120.0 3.4 collective-permute-start.8
  124.8 5.5 %collective-permute-start.10 = (bf16[2,256,256]{1,2,0:T(8,128)(2,1)S(1)}, bf16[2,256,256]{1,2,0:T(8,128)(2,1)S(1)}, u32[]{:S(2)}, u32[]{:S(2)}) collective-permute-start(bf16[2,256,256]{1,2,0:T(8,128)(2,1)S(1)} %pad_maximum_fusion), channel_id=1, source_target_pairs={{0,10},{1,11},{2,12},{3,13},{4,14},{5,15},{6,16},{7,17},{8,18},{9,... | collective-permute-start | bytes 786440 | tf_op jit(solution)/shard_map/ppermute | solution.py:21
  130.3 16.4 %collective-permute-start.11 = (bf16[2,256,256]{1,2,0:T(8,128)(2,1)S(1)}, bf16[2,256,256]{1,2,0:T(8,128)(2,1)S(1)}, u32[]{:S(2)}, u32[]{:S(2)}) collective-permute-start(bf16[2,256,256]{1,2,0:T(8,128)(2,1)S(1)} %pad_maximum_fusion), channel_id=1, source_target_pairs={{0,11},{1,12},{2,13},{3,14},{4,15},{5,16},{6,17},{7,18},{8,19},{9,... | collective-permute-start | bytes 786440 | tf_op jit(solution)/shard_map/ppermute | solution.py:21
  146.7 2.8 collective-permute-start.12
  149.6 4.5 %collective-permute-start.13 = (bf16[2,256,256]{1,2,0:T(8,128)(2,1)S(1)}, bf16[2,256,256]{1,2,0:T(8,128)(2,1)S(1)}, u32[]{:S(2)}, u32[]{:S(2)}) collective-permute-start(bf16[2,256,256]{1,2,0:T(8,128)(2,1)S(1)} %pad_maximum_fusion), channel_id=1, source_target_pairs={{0,13},{1,14},{2,15},{3,16},{4,17},{5,18},{6,19},{7,20},{8,21},{9,... | collective-permute-start | bytes 786440 | tf_op jit(solution)/shard_map/ppermute | solution.py:21
  154.1 5.3 %collective-permute-start.14 = (bf16[2,256,256]{1,2,0:T(8,128)(2,1)S(1)}, bf16[2,256,256]{1,2,0:T(8,128)(2,1)S(1)}, u32[]{:S(2)}, u32[]{:S(2)}) collective-permute-start(bf16[2,256,256]{1,2,0:T(8,128)(2,1)S(1)} %pad_maximum_fusion), channel_id=1, source_target_pairs={{0,14},{1,15},{2,16},{3,17},{4,18},{5,19},{6,20},{7,21},{8,22},{9,... | collective-permute-start | bytes 786440 | tf_op jit(solution)/shard_map/ppermute | solution.py:21
  159.5 13.2 %collective-permute-start.15 = (bf16[2,256,256]{1,2,0:T(8,128)(2,1)S(1)}, bf16[2,256,256]{1,2,0:T(8,128)(2,1)S(1)}, u32[]{:S(2)}, u32[]{:S(2)}) collective-permute-start(bf16[2,256,256]{1,2,0:T(8,128)(2,1)S(1)} %pad_maximum_fusion), channel_id=1, source_target_pairs={{0,15},{1,16},{2,17},{3,18},{4,19},{5,20},{6,21},{7,22},{8,23},{9,... | collective-permute-start | bytes 786440 | tf_op jit(solution)/shard_map/ppermute | solution.py:21
  172.8 30.3 %collective-permute-start.16 = (bf16[2,256,256]{1,2,0:T(8,128)(2,1)S(1)}, bf16[2,256,256]{1,2,0:T(8,128)(2,1)S(1)}, u32[]{:S(2)}, u32[]{:S(2)}) collective-permute-start(bf16[2,256,256]{1,2,0:T(8,128)(2,1)S(1)} %pad_maximum_fusion), channel_id=1, source_target_pairs={{0,16},{1,17},{2,18},{3,19},{4,20},{5,21},{6,22},{7,23},{8,24},{9,... | collective-permute-start | bytes 786440 | tf_op jit(solution)/shard_map/ppermute | solution.py:21
  203.2 7.7 %collective-permute-done.15 = bf16[2,256,256]{1,2,0:T(8,128)(2,1)S(1)} collective-permute-done((bf16[2,256,256]{1,2,0:T(8,128)(2,1)S(1)}, bf16[2,256,256]{1,2,0:T(8,128)(2,1)S(1)}, u32[]{:S(2)}, u32[]{:S(2)}) %collective-permute-start.15) | collective-permute-done | bytes 262176 | tf_op jit(solution)/shard_map/ppermute | solution.py:21
  210.9 5.6 %collective-permute-done.16 = bf16[2,256,256]{1,2,0:T(8,128)(2,1)S(1)} collective-permute-done((bf16[2,256,256]{1,2,0:T(8,128)(2,1)S(1)}, bf16[2,256,256]{1,2,0:T(8,128)(2,1)S(1)}, u32[]{:S(2)}, u32[]{:S(2)}) %collective-permute-start.16) | collective-permute-done | bytes 262176 | tf_op jit(solution)/shard_map/ppermute | solution.py:21
  218.9 4.1 %copy.25 = bf16[17,1,256,256]{3,2,0,1:T(8,128)(2,1)} copy(bf16[17,1,256,256]{2,3,1,0:T(8,128)(2,1)} %get-tuple-element.5) | data formatting | bytes 4456448 | tf_op jit(solution)/shard_map/slice | solution.py:102
  223.0 4.1 %copy.26 = bf16[17,1,256,256]{3,2,0,1:T(8,128)(2,1)} copy(bf16[17,1,256,256]{2,3,1,0:T(8,128)(2,1)} %get-tuple-element.6) | data formatting | bytes 4456448 | tf_op jit(solution)/shard_map/slice | solution.py:103
  227.1 3.3 fusion.52
  233.2 6.4 %fusion.12 = f32[256,2560]{1,0:T(8,128)} fusion(bf16[256,2560]{1,0:T(8,128)(2,1)S(1)} %copy-done, bf16[4352,256]{1,0:T(8,128)(2,1)} %bitcast.54, f32[256,4352]{1,0:T(8,128)} %copy-done.3, f32[256]{0:T(256)S(1)} %fusion.1, f32[256]{0:T(256)S(1)} %get-tuple-element.17), kind=kOutput, calls=%fused_computation.23 | convolution fusion | flops 909377536 | bytes 10618880 | tf_op jit(solution)/shard_map/dot_general | solution.py:123
  241.1 145.7 %all-reduce.2.cloned.1.call-done = f32[256,2560]{1,0:T(8,128)} async-done(((f32[256,2560]{1,0:T(8,128)}), f32[256,2560]{1,0:T(8,128)}) %all-reduce.2.cloned.1.call-update) | async-done | bytes 2621456 | tf_op jit(solution)/shard_map/psum | solution.py:124
  390.0 4.1 %copy.29 = bf16[320,8,2,640]{3,1,2,0:T(8,128)(2,1)S(1)} copy(bf16[320,8,2,640]{3,2,1,0:T(2,128)(2,1)} %bitcast.52) | data formatting | bytes 13107200
  (107 shorter events, 27.4 us)
Async XLA Ops:
  8.0 225.2 %copy-start = (bf16[256,2560]{1,0:T(8,128)(2,1)S(1)}, bf16[256,2560]{1,0:T(8,128)(2,1)}, u32[]{:S(2)}) copy-start(bf16[256,2560]{1,0:T(8,128)(2,1)} %param.15) | copy-start | bytes 3932164
  8.0 54.5 %copy-start.9 = (f32[2560]{0:T(1024)S(1)}, f32[2560]{0:T(1024)}, u32[]{:S(2)}) copy-start(f32[2560]{0:T(1024)} %param.17) | copy-start | bytes 30724
  8.0 52.6 %all-gather.3.cloned.1.call-start = ((), (), s32[]{:S(2)}) async-start(), calls=%async_computation | async-start | bytes 1474560 | tf_op jit(solution)/shard_map/all_gather | solution.py:70
  8.8 378.0 %all-reduce.2.cloned.1.call-start = ((), (), s32[]{:S(2)}) async-start(), calls=%async_computation.1 | async-start | bytes 5242880 | tf_op jit(solution)/shard_map/psum | solution.py:124
  64.7 6.9 %collective-permute-start = (bf16[256,256]{0,1:T(8,128)(2,1)S(1)}, bf16[256,256]{0,1:T(8,128)(2,1)S(1)}, u32[]{:S(2)}, u32[]{:S(2)}) collective-permute-start(bf16[256,256]{0,1:T(8,128)(2,1)S(1)} %convolution_convert_fusion), channel_id=1, source_target_pairs={{0,64},{64,0},{128,192},{192,128},{1,65},{65,1},{129,193},{193,129... | collective-permute-start | bytes 393224 | tf_op jit(solution)/shard_map/ppermute | solution.py:15
  72.5 22.6 %collective-permute-start.1 = (bf16[2,256,256]{1,2,0:T(8,128)(2,1)S(1)}, bf16[2,256,256]{1,2,0:T(8,128)(2,1)S(1)}, u32[]{:S(2)}, u32[]{:S(2)}) collective-permute-start(bf16[2,256,256]{1,2,0:T(8,128)(2,1)S(1)} %pad_maximum_fusion), channel_id=1, source_target_pairs={{0,1},{1,2},{2,3},{3,4},{4,5},{5,6},{6,7},{7,8},{8,9},{9,10},{10,1... | collective-permute-start | bytes 786440 | tf_op jit(solution)/shard_map/ppermute | solution.py:21
  75.0 26.2 %collective-permute-start.2 = (bf16[2,256,256]{1,2,0:T(8,128)(2,1)S(1)}, bf16[2,256,256]{1,2,0:T(8,128)(2,1)S(1)}, u32[]{:S(2)}, u32[]{:S(2)}) collective-permute-start(bf16[2,256,256]{1,2,0:T(8,128)(2,1)S(1)} %pad_maximum_fusion), channel_id=1, source_target_pairs={{0,2},{1,3},{2,4},{3,5},{4,6},{5,7},{6,8},{7,9},{8,10},{9,11},{10,... | collective-permute-start | bytes 786440 | tf_op jit(solution)/shard_map/ppermute | solution.py:21
  79.6 40.3 %collective-permute-start.3 = (bf16[2,256,256]{1,2,0:T(8,128)(2,1)S(1)}, bf16[2,256,256]{1,2,0:T(8,128)(2,1)S(1)}, u32[]{:S(2)}, u32[]{:S(2)}) collective-permute-start(bf16[2,256,256]{1,2,0:T(8,128)(2,1)S(1)} %pad_maximum_fusion), channel_id=1, source_target_pairs={{0,3},{1,4},{2,5},{3,6},{4,7},{5,8},{6,9},{7,10},{8,11},{9,12},{10... | collective-permute-start | bytes 786440 | tf_op jit(solution)/shard_map/ppermute | solution.py:21
  84.9 38.5 %collective-permute-start.4 = (bf16[2,256,256]{1,2,0:T(8,128)(2,1)S(1)}, bf16[2,256,256]{1,2,0:T(8,128)(2,1)S(1)}, u32[]{:S(2)}, u32[]{:S(2)}) collective-permute-start(bf16[2,256,256]{1,2,0:T(8,128)(2,1)S(1)} %pad_maximum_fusion), channel_id=1, source_target_pairs={{0,4},{1,5},{2,6},{3,7},{4,8},{5,9},{6,10},{7,11},{8,12},{9,13},{1... | collective-permute-start | bytes 786440 | tf_op jit(solution)/shard_map/ppermute | solution.py:21
  90.3 34.4 %collective-permute-start.5 = (bf16[2,256,256]{1,2,0:T(8,128)(2,1)S(1)}, bf16[2,256,256]{1,2,0:T(8,128)(2,1)S(1)}, u32[]{:S(2)}, u32[]{:S(2)}) collective-permute-start(bf16[2,256,256]{1,2,0:T(8,128)(2,1)S(1)} %pad_maximum_fusion), channel_id=1, source_target_pairs={{0,5},{1,6},{2,7},{3,8},{4,9},{5,10},{6,11},{7,12},{8,13},{9,14},{... | collective-permute-start | bytes 786440 | tf_op jit(solution)/shard_map/ppermute | solution.py:21
  95.1 35.2 %collective-permute-start.6 = (bf16[2,256,256]{1,2,0:T(8,128)(2,1)S(1)}, bf16[2,256,256]{1,2,0:T(8,128)(2,1)S(1)}, u32[]{:S(2)}, u32[]{:S(2)}) collective-permute-start(bf16[2,256,256]{1,2,0:T(8,128)(2,1)S(1)} %pad_maximum_fusion), channel_id=1, source_target_pairs={{0,6},{1,7},{2,8},{3,9},{4,10},{5,11},{6,12},{7,13},{8,14},{9,15},... | collective-permute-start | bytes 786440 | tf_op jit(solution)/shard_map/ppermute | solution.py:21
  101.2 45.6 %collective-permute-start.7 = (bf16[2,256,256]{1,2,0:T(8,128)(2,1)S(1)}, bf16[2,256,256]{1,2,0:T(8,128)(2,1)S(1)}, u32[]{:S(2)}, u32[]{:S(2)}) collective-permute-start(bf16[2,256,256]{1,2,0:T(8,128)(2,1)S(1)} %pad_maximum_fusion), channel_id=1, source_target_pairs={{0,7},{1,8},{2,9},{3,10},{4,11},{5,12},{6,13},{7,14},{8,15},{9,16}... | collective-permute-start | bytes 786440 | tf_op jit(solution)/shard_map/ppermute | solution.py:21
  120.0 29.6 %collective-permute-start.8 = (bf16[2,256,256]{1,2,0:T(8,128)(2,1)S(1)}, bf16[2,256,256]{1,2,0:T(8,128)(2,1)S(1)}, u32[]{:S(2)}, u32[]{:S(2)}) collective-permute-start(bf16[2,256,256]{1,2,0:T(8,128)(2,1)S(1)} %pad_maximum_fusion), channel_id=1, source_target_pairs={{0,8},{1,9},{2,10},{3,11},{4,12},{5,13},{6,14},{7,15},{8,16},{9,17... | collective-permute-start | bytes 786440 | tf_op jit(solution)/shard_map/ppermute | solution.py:21
  123.4 30.7 %collective-permute-start.9 = (bf16[2,256,256]{1,2,0:T(8,128)(2,1)S(1)}, bf16[2,256,256]{1,2,0:T(8,128)(2,1)S(1)}, u32[]{:S(2)}, u32[]{:S(2)}) collective-permute-start(bf16[2,256,256]{1,2,0:T(8,128)(2,1)S(1)} %pad_maximum_fusion), channel_id=1, source_target_pairs={{0,9},{1,10},{2,11},{3,12},{4,13},{5,14},{6,15},{7,16},{8,17},{9,1... | collective-permute-start | bytes 786440 | tf_op jit(solution)/shard_map/ppermute | solution.py:21
  124.8 34.7 %collective-permute-start.10 = (bf16[2,256,256]{1,2,0:T(8,128)(2,1)S(1)}, bf16[2,256,256]{1,2,0:T(8,128)(2,1)S(1)}, u32[]{:S(2)}, u32[]{:S(2)}) collective-permute-start(bf16[2,256,256]{1,2,0:T(8,128)(2,1)S(1)} %pad_maximum_fusion), channel_id=1, source_target_pairs={{0,10},{1,11},{2,12},{3,13},{4,14},{5,15},{6,16},{7,17},{8,18},{9,... | collective-permute-start | bytes 786440 | tf_op jit(solution)/shard_map/ppermute | solution.py:21
  130.3 42.5 %collective-permute-start.11 = (bf16[2,256,256]{1,2,0:T(8,128)(2,1)S(1)}, bf16[2,256,256]{1,2,0:T(8,128)(2,1)S(1)}, u32[]{:S(2)}, u32[]{:S(2)}) collective-permute-start(bf16[2,256,256]{1,2,0:T(8,128)(2,1)S(1)} %pad_maximum_fusion), channel_id=1, source_target_pairs={{0,11},{1,12},{2,13},{3,14},{4,15},{5,16},{6,17},{7,18},{8,19},{9,... | collective-permute-start | bytes 786440 | tf_op jit(solution)/shard_map/ppermute | solution.py:21
  146.7 56.4 %collective-permute-start.12 = (bf16[2,256,256]{1,2,0:T(8,128)(2,1)S(1)}, bf16[2,256,256]{1,2,0:T(8,128)(2,1)S(1)}, u32[]{:S(2)}, u32[]{:S(2)}) collective-permute-start(bf16[2,256,256]{1,2,0:T(8,128)(2,1)S(1)} %pad_maximum_fusion), channel_id=1, source_target_pairs={{0,12},{1,13},{2,14},{3,15},{4,16},{5,17},{6,18},{7,19},{8,20},{9,... | collective-permute-start | bytes 786440 | tf_op jit(solution)/shard_map/ppermute | solution.py:21
  149.6 53.6 %collective-permute-start.13 = (bf16[2,256,256]{1,2,0:T(8,128)(2,1)S(1)}, bf16[2,256,256]{1,2,0:T(8,128)(2,1)S(1)}, u32[]{:S(2)}, u32[]{:S(2)}) collective-permute-start(bf16[2,256,256]{1,2,0:T(8,128)(2,1)S(1)} %pad_maximum_fusion), channel_id=1, source_target_pairs={{0,13},{1,14},{2,15},{3,16},{4,17},{5,18},{6,19},{7,20},{8,21},{9,... | collective-permute-start | bytes 786440 | tf_op jit(solution)/shard_map/ppermute | solution.py:21
  154.1 49.1 %collective-permute-start.14 = (bf16[2,256,256]{1,2,0:T(8,128)(2,1)S(1)}, bf16[2,256,256]{1,2,0:T(8,128)(2,1)S(1)}, u32[]{:S(2)}, u32[]{:S(2)}) collective-permute-start(bf16[2,256,256]{1,2,0:T(8,128)(2,1)S(1)} %pad_maximum_fusion), channel_id=1, source_target_pairs={{0,14},{1,15},{2,16},{3,17},{4,18},{5,19},{6,20},{7,21},{8,22},{9,... | collective-permute-start | bytes 786440 | tf_op jit(solution)/shard_map/ppermute | solution.py:21
  159.5 51.4 %collective-permute-start.15 = (bf16[2,256,256]{1,2,0:T(8,128)(2,1)S(1)}, bf16[2,256,256]{1,2,0:T(8,128)(2,1)S(1)}, u32[]{:S(2)}, u32[]{:S(2)}) collective-permute-start(bf16[2,256,256]{1,2,0:T(8,128)(2,1)S(1)} %pad_maximum_fusion), channel_id=1, source_target_pairs={{0,15},{1,16},{2,17},{3,18},{4,19},{5,20},{6,21},{7,22},{8,23},{9,... | collective-permute-start | bytes 786440 | tf_op jit(solution)/shard_map/ppermute | solution.py:21
  172.8 43.8 %collective-permute-start.16 = (bf16[2,256,256]{1,2,0:T(8,128)(2,1)S(1)}, bf16[2,256,256]{1,2,0:T(8,128)(2,1)S(1)}, u32[]{:S(2)}, u32[]{:S(2)}) collective-permute-start(bf16[2,256,256]{1,2,0:T(8,128)(2,1)S(1)} %pad_maximum_fusion), channel_id=1, source_target_pairs={{0,16},{1,17},{2,18},{3,19},{4,20},{5,21},{6,22},{7,23},{8,24},{9,... | collective-permute-start | bytes 786440 | tf_op jit(solution)/shard_map/ppermute | solution.py:21
  239.6 149.3 %copy-start.5 = (f32[2560]{0:T(1024)S(1)}, f32[2560]{0:T(1024)}, u32[]{:S(2)}) copy-start(f32[2560]{0:T(1024)} %param.18) | copy-start | bytes 30724
  239.6 150.4 %all-gather.5.cloned.1.call-start = ((), (), s32[]{:S(2)}) async-start(), calls=%async_computation.2 | async-start | bytes 6656000 | tf_op jit(solution)/shard_map/all_gather | solution.py:127
  241.0 148.9 %copy-start.4 = (bf16[2,128,256]{2,1,0:T(8,128)(2,1)}, bf16[2,128,256]{2,1,0:T(8,128)(2,1)S(1)}, u32[]{:S(2)}) copy-start(bf16[2,128,256]{2,1,0:T(8,128)(2,1)S(1)} %scatter_fusion) | copy-start | bytes 393220
  (8 other events, 27.8 us)
Sparse Core Ops, SparseCore 0:
  10.9 49.6 all-gather.2
  239.8 146.9 all-reduce.1
Sparse Core Ops, SparseCore 1:
  243.4 133.3 all-gather.4
where the time goes:
time: 406 us; the launch traced here: 405 us
  waiting for transfers between devices  214 us (53%)
  starting transfers between devices  132 us (33%)
  local copies, waits for them, and re-layouts  19.8 us (5%)
  between operations  16.2 us (4%)
  matrix products  14.9 us (4%)
  other arithmetic  8.28 us (2%)
    psum x1, waiting for transfers between devices, local(): attended = lax.psum(head_terms, ('section', 'tensor'))  146 us
    ppermute x16, starting transfers between devices, shifted(): return lax.ppermute(block, axis, route)  130 us
    all_gather x1, waiting for transfers between devices, local(): features = lax.all_gather(tokens, ('section', 'tensor'), axis=1, tiled=True)  49.9 us
    ppermute x16, waiting for transfers between devices, shifted(): return lax.ppermute(block, axis, route)  13.3 us
  transfers between devices with their start and end apart: 20, of which 5 were waited for; matrix products, arithmetic and copies ran while one was open for 2% of the time, Pallas kernels for 0%

commit v1 on v0

--- a/solution.py
+++ b/solution.py
@@ -121,7 +121,7 @@
         jnp.bfloat16
     )
     head_terms = jnp.dot(attention_out, w_out, preferred_element_type=jnp.float32)
-    attended = lax.psum(head_terms, ("section", "tensor"))
+    attended = jnp.sum(lax.all_gather(head_terms, ("section", "tensor")), axis=0)
     residual = features.astype(jnp.float32) + rms_norm(attended, post_gain)
     ffn_input = rms_norm(residual, mlp_gain).astype(jnp.bfloat16)
     row_piece = lax.all_gather(w_gateup, "seq", axis=0, tiled=True)

time: 406 us -> 531 us (1.31)
  the two profiles are of different devices: /device:TPU:8 before, /device:TPU:1 now
where the time goes in v1:
time: 531 us
  waiting for transfers between devices  332 us (63%)
  starting transfers between devices  125 us (24%)
  local copies, waits for them, and re-layouts  22.9 us (4%)
  other arithmetic  18.4 us (3%)
  matrix products  17.9 us (3%)
  between operations  14.4 us (3%)
    all_gather x1, waiting for transfers between devices, local(): lax.all_gather(head_terms, ('section', 'tensor'))  232 us
    ppermute x16, starting transfers between devices, shifted(): return lax.ppermute(block, axis, route)  123 us
    all_gather x1, waiting for transfers between devices, local(): features = lax.all_gather(tokens, ('section', 'tensor'), axis=1, tiled=True)  43.9 us
    all_gather x1, waiting for transfers between devices, local(): row_piece = lax.all_gather(w_gateup, 'seq', axis=0, tiled=True)  27.1 us
    ppermute x16, waiting for transfers between devices, shifted(): return lax.ppermute(block, axis, route)  24.6 us
  transfers between devices with their start and end apart: 20, of which 8 were waited for; matrix products, arithmetic and copies ran while one was open for 7% of the time, Pallas kernels for 0%

profile of v1, /device:TPU:1, one launch (start us, length us, event | category | flops | bytes accessed | tf_op | source)
XLA Modules:
  0.0 530.6 jit_solution(3194436766543461639)
XLA Ops:
  10.6 43.9 %all-gather.5.cloned.1.call-done = bf16[256,2560]{0,1:T(8,128)(2,1)} async-done(((bf16[256,320]{0,1:T(8,128)(2,1)}), bf16[256,2560]{0,1:T(8,128)(2,1)}) %all-gather.5.cloned.1.call-update) | async-done | bytes 1310736 | tf_op jit(solution)/shard_map/all_gather | solution.py:70
  65.3 12.2 %collective-permute-start.1 = (bf16[2,256,256]{1,2,0:T(8,128)(2,1)S(1)}, bf16[2,256,256]{1,2,0:T(8,128)(2,1)S(1)}, u32[]{:S(2)}, u32[]{:S(2)}) collective-permute-start(bf16[2,256,256]{1,2,0:T(8,128)(2,1)S(1)} %pad_maximum_fusion), channel_id=1, source_target_pairs={{0,1},{1,2},{2,3},{3,4},{4,5},{5,6},{6,7},{7,8},{8,9},{9,10},{10,1... | collective-permute-start | bytes 786440 | tf_op jit(solution)/shard_map/ppermute | solution.py:21
  78.0 4.7 collective-permute-start.2
  85.3 5.1 collective-permute-start.4
  90.4 4.5 collective-permute-start.5
  94.9 4.2 collective-permute-start.6
  99.2 5.8 %collective-permute-start.7 = (bf16[2,256,256]{1,2,0:T(8,128)(2,1)S(1)}, bf16[2,256,256]{1,2,0:T(8,128)(2,1)S(1)}, u32[]{:S(2)}, u32[]{:S(2)}) collective-permute-start(bf16[2,256,256]{1,2,0:T(8,128)(2,1)S(1)} %pad_maximum_fusion), channel_id=1, source_target_pairs={{0,7},{1,8},{2,9},{3,10},{4,11},{5,12},{6,13},{7,14},{8,15},{9,16}... | collective-permute-start | bytes 786440 | tf_op jit(solution)/shard_map/ppermute | solution.py:21
  105.0 13.0 %collective-permute-start.8 = (bf16[2,256,256]{1,2,0:T(8,128)(2,1)S(1)}, bf16[2,256,256]{1,2,0:T(8,128)(2,1)S(1)}, u32[]{:S(2)}, u32[]{:S(2)}) collective-permute-start(bf16[2,256,256]{1,2,0:T(8,128)(2,1)S(1)} %pad_maximum_fusion), channel_id=1, source_target_pairs={{0,8},{1,9},{2,10},{3,11},{4,12},{5,13},{6,14},{7,15},{8,16},{9,17... | collective-permute-start | bytes 786440 | tf_op jit(solution)/shard_map/ppermute | solution.py:21
  118.0 8.5 %collective-permute-start.9 = (bf16[2,256,256]{1,2,0:T(8,128)(2,1)S(1)}, bf16[2,256,256]{1,2,0:T(8,128)(2,1)S(1)}, u32[]{:S(2)}, u32[]{:S(2)}) collective-permute-start(bf16[2,256,256]{1,2,0:T(8,128)(2,1)S(1)} %pad_maximum_fusion), channel_id=1, source_target_pairs={{0,9},{1,10},{2,11},{3,12},{4,13},{5,14},{6,15},{7,16},{8,17},{9,1... | collective-permute-start | bytes 786440 | tf_op jit(solution)/shard_map/ppermute | solution.py:21
  126.5 16.7 %collective-permute-start.10 = (bf16[2,256,256]{1,2,0:T(8,128)(2,1)S(1)}, bf16[2,256,256]{1,2,0:T(8,128)(2,1)S(1)}, u32[]{:S(2)}, u32[]{:S(2)}) collective-permute-start(bf16[2,256,256]{1,2,0:T(8,128)(2,1)S(1)} %pad_maximum_fusion), channel_id=1, source_target_pairs={{0,10},{1,11},{2,12},{3,13},{4,14},{5,15},{6,16},{7,17},{8,18},{9,... | collective-permute-start | bytes 786440 | tf_op jit(solution)/shard_map/ppermute | solution.py:21
  143.3 10.0 %collective-permute-start.11 = (bf16[2,256,256]{1,2,0:T(8,128)(2,1)S(1)}, bf16[2,256,256]{1,2,0:T(8,128)(2,1)S(1)}, u32[]{:S(2)}, u32[]{:S(2)}) collective-permute-start(bf16[2,256,256]{1,2,0:T(8,128)(2,1)S(1)} %pad_maximum_fusion), channel_id=1, source_target_pairs={{0,11},{1,12},{2,13},{3,14},{4,15},{5,16},{6,17},{7,18},{8,19},{9,... | collective-permute-start | bytes 786440 | tf_op jit(solution)/shard_map/ppermute | solution.py:21
  160.4 12.3 %collective-permute-start.15 = (bf16[2,256,256]{1,2,0:T(8,128)(2,1)S(1)}, bf16[2,256,256]{1,2,0:T(8,128)(2,1)S(1)}, u32[]{:S(2)}, u32[]{:S(2)}) collective-permute-start(bf16[2,256,256]{1,2,0:T(8,128)(2,1)S(1)} %pad_maximum_fusion), channel_id=1, source_target_pairs={{0,15},{1,16},{2,17},{3,18},{4,19},{5,20},{6,21},{7,22},{8,23},{9,... | collective-permute-start | bytes 786440 | tf_op jit(solution)/shard_map/ppermute | solution.py:21
  172.8 16.7 %collective-permute-start.16 = (bf16[2,256,256]{1,2,0:T(8,128)(2,1)S(1)}, bf16[2,256,256]{1,2,0:T(8,128)(2,1)S(1)}, u32[]{:S(2)}, u32[]{:S(2)}) collective-permute-start(bf16[2,256,256]{1,2,0:T(8,128)(2,1)S(1)} %pad_maximum_fusion), channel_id=1, source_target_pairs={{0,16},{1,17},{2,18},{3,19},{4,20},{5,21},{6,22},{7,23},{8,24},{9,... | collective-permute-start | bytes 786440 | tf_op jit(solution)/shard_map/ppermute | solution.py:21
  191.2 12.2 %collective-permute-done.14 = bf16[2,256,256]{1,2,0:T(8,128)(2,1)S(1)} collective-permute-done((bf16[2,256,256]{1,2,0:T(8,128)(2,1)S(1)}, bf16[2,256,256]{1,2,0:T(8,128)(2,1)S(1)}, u32[]{:S(2)}, u32[]{:S(2)}) %collective-permute-start.14) | collective-permute-done | bytes 262176 | tf_op jit(solution)/shard_map/ppermute | solution.py:21
  203.5 5.9 %collective-permute-done.15 = bf16[2,256,256]{1,2,0:T(8,128)(2,1)S(1)} collective-permute-done((bf16[2,256,256]{1,2,0:T(8,128)(2,1)S(1)}, bf16[2,256,256]{1,2,0:T(8,128)(2,1)S(1)}, u32[]{:S(2)}, u32[]{:S(2)}) %collective-permute-start.15) | collective-permute-done | bytes 262176 | tf_op jit(solution)/shard_map/ppermute | solution.py:21
  209.4 4.8 collective-permute-done.16
  216.5 4.1 copy.27
  220.6 4.1 copy.28
  230.8 6.5 %fusion.12 = f32[256,2560]{1,0:T(8,128)} fusion(bf16[256,2560]{1,0:T(8,128)(2,1)S(1)} %copy-done, bf16[4352,256]{1,0:T(8,128)(2,1)} %bitcast.56, f32[256,4352]{1,0:T(8,128)} %copy-done.3, f32[256]{0:T(256)S(1)} %fusion.1, f32[256]{0:T(256)S(1)} %get-tuple-element.17), kind=kOutput, calls=%fused_computation.23 | convolution fusion | flops 909377536 | bytes 10618880 | tf_op jit(solution)/shard_map/dot_general | solution.py:123
  238.8 27.1 %all-gather.7.cloned.1.call-done = bf16[2560,2,640]{2,1,0:T(2,128)(2,1)} async-done(((bf16[40,2,640]{2,1,0:T(2,128)(2,1)}), bf16[2560,2,640]{2,1,0:T(2,128)(2,1)}) %all-gather.7.cloned.1.call-update) | async-done | bytes 6553616 | tf_op jit(solution)/shard_map/all_gather | solution.py:127
  265.9 6.7 %copy.31 = bf16[320,8,2,640]{3,1,2,0:T(8,128)(2,1)} copy(bf16[320,8,2,640]{3,2,1,0:T(2,128)(2,1)} %bitcast.54) | data formatting | bytes 13107200
  272.6 232.0 %all-gather.9.cloned.1.call-done = f32[2048,2560]{1,0:T(8,128)} async-done(((f32[256,2560]{1,0:T(8,128)}), f32[2048,2560]{1,0:T(8,128)}) %all-gather.9.cloned.1.call-update) | async-done | bytes 20971536 | tf_op jit(solution)/shard_map/all_gather | solution.py:124
  504.5 10.2 %reduce_sum.97 = f32[256,2560]{1,0:T(8,128)} reduce(f32[8,256,2560]{2,1,0:T(8,128)} %bitcast.53, f32[]{:T(128)} %constant.18.clone.1), dimensions={0}, to_apply=%region_9.10 | reduce | flops 4587520 | bytes 23592964 | tf_op jit(solution)/shard_map/reduce_sum | solution.py:124
  518.0 5.1 fusion.6
  (108 shorter events, 40.0 us)
Async XLA Ops:
  7.2 223.7 %copy-start = (bf16[256,2560]{1,0:T(8,128)(2,1)S(1)}, bf16[256,2560]{1,0:T(8,128)(2,1)}, u32[]{:S(2)}) copy-start(bf16[256,2560]{1,0:T(8,128)(2,1)} %param.15) | copy-start | bytes 3932164
  7.2 49.3 %copy-start.9 = (f32[2560]{0:T(1024)S(1)}, f32[2560]{0:T(1024)}, u32[]{:S(2)}) copy-start(f32[2560]{0:T(1024)} %param.17) | copy-start | bytes 30724
  7.2 47.4 %all-gather.5.cloned.1.call-start = ((), (), s32[]{:S(2)}) async-start(), calls=%async_computation | async-start | bytes 1474560 | tf_op jit(solution)/shard_map/all_gather | solution.py:70
  7.9 258.0 %all-gather.7.cloned.1.call-start = ((), (), s32[]{:S(2)}) async-start(), calls=%async_computation.1 | async-start | bytes 6656000 | tf_op jit(solution)/shard_map/all_gather | solution.py:127
  8.7 495.9 %all-gather.9.cloned.1.call-start = ((), (), s32[]{:S(2)}) async-start(), calls=%async_computation.2 | async-start | bytes 23592960 | tf_op jit(solution)/shard_map/all_gather | solution.py:124
  58.7 5.7 %collective-permute-start = (bf16[256,256]{0,1:T(8,128)(2,1)S(1)}, bf16[256,256]{0,1:T(8,128)(2,1)S(1)}, u32[]{:S(2)}, u32[]{:S(2)}) collective-permute-start(bf16[256,256]{0,1:T(8,128)(2,1)S(1)} %convolution_convert_fusion), channel_id=1, source_target_pairs={{0,64},{64,0},{128,192},{192,128},{1,65},{65,1},{129,193},{193,129... | collective-permute-start | bytes 393224 | tf_op jit(solution)/shard_map/ppermute | solution.py:15
  65.3 29.7 %collective-permute-start.1 = (bf16[2,256,256]{1,2,0:T(8,128)(2,1)S(1)}, bf16[2,256,256]{1,2,0:T(8,128)(2,1)S(1)}, u32[]{:S(2)}, u32[]{:S(2)}) collective-permute-start(bf16[2,256,256]{1,2,0:T(8,128)(2,1)S(1)} %pad_maximum_fusion), channel_id=1, source_target_pairs={{0,1},{1,2},{2,3},{3,4},{4,5},{5,6},{6,7},{7,8},{8,9},{9,10},{10,1... | collective-permute-start | bytes 786440 | tf_op jit(solution)/shard_map/ppermute | solution.py:21
  78.0 21.1 %collective-permute-start.2 = (bf16[2,256,256]{1,2,0:T(8,128)(2,1)S(1)}, bf16[2,256,256]{1,2,0:T(8,128)(2,1)S(1)}, u32[]{:S(2)}, u32[]{:S(2)}) collective-permute-start(bf16[2,256,256]{1,2,0:T(8,128)(2,1)S(1)} %pad_maximum_fusion), channel_id=1, source_target_pairs={{0,2},{1,3},{2,4},{3,5},{4,6},{5,7},{6,8},{7,9},{8,10},{9,11},{10,... | collective-permute-start | bytes 786440 | tf_op jit(solution)/shard_map/ppermute | solution.py:21
  82.7 22.2 %collective-permute-start.3 = (bf16[2,256,256]{1,2,0:T(8,128)(2,1)S(1)}, bf16[2,256,256]{1,2,0:T(8,128)(2,1)S(1)}, u32[]{:S(2)}, u32[]{:S(2)}) collective-permute-start(bf16[2,256,256]{1,2,0:T(8,128)(2,1)S(1)} %pad_maximum_fusion), channel_id=1, source_target_pairs={{0,3},{1,4},{2,5},{3,6},{4,7},{5,8},{6,9},{7,10},{8,11},{9,12},{10... | collective-permute-start | bytes 786440 | tf_op jit(solution)/shard_map/ppermute | solution.py:21
  85.3 32.7 %collective-permute-start.4 = (bf16[2,256,256]{1,2,0:T(8,128)(2,1)S(1)}, bf16[2,256,256]{1,2,0:T(8,128)(2,1)S(1)}, u32[]{:S(2)}, u32[]{:S(2)}) collective-permute-start(bf16[2,256,256]{1,2,0:T(8,128)(2,1)S(1)} %pad_maximum_fusion), channel_id=1, source_target_pairs={{0,4},{1,5},{2,6},{3,7},{4,8},{5,9},{6,10},{7,11},{8,12},{9,13},{1... | collective-permute-start | bytes 786440 | tf_op jit(solution)/shard_map/ppermute | solution.py:21
  90.4 36.1 %collective-permute-start.5 = (bf16[2,256,256]{1,2,0:T(8,128)(2,1)S(1)}, bf16[2,256,256]{1,2,0:T(8,128)(2,1)S(1)}, u32[]{:S(2)}, u32[]{:S(2)}) collective-permute-start(bf16[2,256,256]{1,2,0:T(8,128)(2,1)S(1)} %pad_maximum_fusion), channel_id=1, source_target_pairs={{0,5},{1,6},{2,7},{3,8},{4,9},{5,10},{6,11},{7,12},{8,13},{9,14},{... | collective-permute-start | bytes 786440 | tf_op jit(solution)/shard_map/ppermute | solution.py:21
  94.9 48.4 %collective-permute-start.6 = (bf16[2,256,256]{1,2,0:T(8,128)(2,1)S(1)}, bf16[2,256,256]{1,2,0:T(8,128)(2,1)S(1)}, u32[]{:S(2)}, u32[]{:S(2)}) collective-permute-start(bf16[2,256,256]{1,2,0:T(8,128)(2,1)S(1)} %pad_maximum_fusion), channel_id=1, source_target_pairs={{0,6},{1,7},{2,8},{3,9},{4,10},{5,11},{6,12},{7,13},{8,14},{9,15},... | collective-permute-start | bytes 786440 | tf_op jit(solution)/shard_map/ppermute | solution.py:21
  99.2 54.2 %collective-permute-start.7 = (bf16[2,256,256]{1,2,0:T(8,128)(2,1)S(1)}, bf16[2,256,256]{1,2,0:T(8,128)(2,1)S(1)}, u32[]{:S(2)}, u32[]{:S(2)}) collective-permute-start(bf16[2,256,256]{1,2,0:T(8,128)(2,1)S(1)} %pad_maximum_fusion), channel_id=1, source_target_pairs={{0,7},{1,8},{2,9},{3,10},{4,11},{5,12},{6,13},{7,14},{8,15},{9,16}... | collective-permute-start | bytes 786440 | tf_op jit(solution)/shard_map/ppermute | solution.py:21
  105.0 52.0 %collective-permute-start.8 = (bf16[2,256,256]{1,2,0:T(8,128)(2,1)S(1)}, bf16[2,256,256]{1,2,0:T(8,128)(2,1)S(1)}, u32[]{:S(2)}, u32[]{:S(2)}) collective-permute-start(bf16[2,256,256]{1,2,0:T(8,128)(2,1)S(1)} %pad_maximum_fusion), channel_id=1, source_target_pairs={{0,8},{1,9},{2,10},{3,11},{4,12},{5,13},{6,14},{7,15},{8,16},{9,17... | collective-permute-start | bytes 786440 | tf_op jit(solution)/shard_map/ppermute | solution.py:21
  118.0 40.4 %collective-permute-start.9 = (bf16[2,256,256]{1,2,0:T(8,128)(2,1)S(1)}, bf16[2,256,256]{1,2,0:T(8,128)(2,1)S(1)}, u32[]{:S(2)}, u32[]{:S(2)}) collective-permute-start(bf16[2,256,256]{1,2,0:T(8,128)(2,1)S(1)} %pad_maximum_fusion), channel_id=1, source_target_pairs={{0,9},{1,10},{2,11},{3,12},{4,13},{5,14},{6,15},{7,16},{8,17},{9,1... | collective-permute-start | bytes 786440 | tf_op jit(solution)/shard_map/ppermute | solution.py:21
  126.5 33.9 %collective-permute-start.10 = (bf16[2,256,256]{1,2,0:T(8,128)(2,1)S(1)}, bf16[2,256,256]{1,2,0:T(8,128)(2,1)S(1)}, u32[]{:S(2)}, u32[]{:S(2)}) collective-permute-start(bf16[2,256,256]{1,2,0:T(8,128)(2,1)S(1)} %pad_maximum_fusion), channel_id=1, source_target_pairs={{0,10},{1,11},{2,12},{3,13},{4,14},{5,15},{6,16},{7,17},{8,18},{9,... | collective-permute-start | bytes 786440 | tf_op jit(solution)/shard_map/ppermute | solution.py:21
  143.3 29.5 %collective-permute-start.11 = (bf16[2,256,256]{1,2,0:T(8,128)(2,1)S(1)}, bf16[2,256,256]{1,2,0:T(8,128)(2,1)S(1)}, u32[]{:S(2)}, u32[]{:S(2)}) collective-permute-start(bf16[2,256,256]{1,2,0:T(8,128)(2,1)S(1)} %pad_maximum_fusion), channel_id=1, source_target_pairs={{0,11},{1,12},{2,13},{3,14},{4,15},{5,16},{6,17},{7,18},{8,19},{9,... | collective-permute-start | bytes 786440 | tf_op jit(solution)/shard_map/ppermute | solution.py:21
  153.4 36.1 %collective-permute-start.12 = (bf16[2,256,256]{1,2,0:T(8,128)(2,1)S(1)}, bf16[2,256,256]{1,2,0:T(8,128)(2,1)S(1)}, u32[]{:S(2)}, u32[]{:S(2)}) collective-permute-start(bf16[2,256,256]{1,2,0:T(8,128)(2,1)S(1)} %pad_maximum_fusion), channel_id=1, source_target_pairs={{0,12},{1,13},{2,14},{3,15},{4,16},{5,17},{6,18},{7,19},{8,20},{9,... | collective-permute-start | bytes 786440 | tf_op jit(solution)/shard_map/ppermute | solution.py:21
  157.0 34.2 %collective-permute-start.13 = (bf16[2,256,256]{1,2,0:T(8,128)(2,1)S(1)}, bf16[2,256,256]{1,2,0:T(8,128)(2,1)S(1)}, u32[]{:S(2)}, u32[]{:S(2)}) collective-permute-start(bf16[2,256,256]{1,2,0:T(8,128)(2,1)S(1)} %pad_maximum_fusion), channel_id=1, source_target_pairs={{0,13},{1,14},{2,15},{3,16},{4,17},{5,18},{6,19},{7,20},{8,21},{9,... | collective-permute-start | bytes 786440 | tf_op jit(solution)/shard_map/ppermute | solution.py:21
  158.4 45.1 %collective-permute-start.14 = (bf16[2,256,256]{1,2,0:T(8,128)(2,1)S(1)}, bf16[2,256,256]{1,2,0:T(8,128)(2,1)S(1)}, u32[]{:S(2)}, u32[]{:S(2)}) collective-permute-start(bf16[2,256,256]{1,2,0:T(8,128)(2,1)S(1)} %pad_maximum_fusion), channel_id=1, source_target_pairs={{0,14},{1,15},{2,16},{3,17},{4,18},{5,19},{6,20},{7,21},{8,22},{9,... | collective-permute-start | bytes 786440 | tf_op jit(solution)/shard_map/ppermute | solution.py:21
  160.4 49.0 %collective-permute-start.15 = (bf16[2,256,256]{1,2,0:T(8,128)(2,1)S(1)}, bf16[2,256,256]{1,2,0:T(8,128)(2,1)S(1)}, u32[]{:S(2)}, u32[]{:S(2)}) collective-permute-start(bf16[2,256,256]{1,2,0:T(8,128)(2,1)S(1)} %pad_maximum_fusion), channel_id=1, source_target_pairs={{0,15},{1,16},{2,17},{3,18},{4,19},{5,20},{6,21},{7,22},{8,23},{9,... | collective-permute-start | bytes 786440 | tf_op jit(solution)/shard_map/ppermute | solution.py:21
  172.8 41.4 %collective-permute-start.16 = (bf16[2,256,256]{1,2,0:T(8,128)(2,1)S(1)}, bf16[2,256,256]{1,2,0:T(8,128)(2,1)S(1)}, u32[]{:S(2)}, u32[]{:S(2)}) collective-permute-start(bf16[2,256,256]{1,2,0:T(8,128)(2,1)S(1)} %pad_maximum_fusion), channel_id=1, source_target_pairs={{0,16},{1,17},{2,18},{3,19},{4,20},{5,21},{6,22},{7,23},{8,24},{9,... | collective-permute-start | bytes 786440 | tf_op jit(solution)/shard_map/ppermute | solution.py:21
  238.8 33.8 %copy-start.4 = (bf16[2,128,256]{2,1,0:T(8,128)(2,1)}, bf16[2,128,256]{2,1,0:T(8,128)(2,1)S(1)}, u32[]{:S(2)}) copy-start(bf16[2,128,256]{2,1,0:T(8,128)(2,1)S(1)} %scatter_fusion) | copy-start | bytes 393220
  504.5 12.3 %copy-start.5 = (f32[2560]{0:T(1024)S(1)}, f32[2560]{0:T(1024)}, u32[]{:S(2)}) copy-start(f32[2560]{0:T(1024)} %param.18) | copy-start | bytes 30724
  (8 other events, 25.8 us)
Sparse Core Ops, SparseCore 0:
  10.1 44.4 all-gather.4
  57.8 208.0 all-gather.6
  268.0 236.5 all-gather.8
